TPU v7x, 256 devices: a whole 4x4x8 slice. The times are simulated.
256 devices in a mesh: blk: 64 (over y, z, core), lev: 4 (over x).
Axes of the slice: x: 4, y: 4, z: 8, core: 2. Of those that a mesh axis runs over, the one named last changes fastest.
Arguments:
- adjoint_in: float32 [4096, 12, 1024], P('blk', 'lev'), may hold values from -6 to 6
- courant: float32 [2, 4096, 12, 1024], P(None, 'blk', 'lev'), may hold values from 0.05 to 0.45
- mixing: float32 [4096, 12, 1024], P('blk', 'lev'), may hold values from 0.5 to 8
- oh_rate: float32 [4096, 12, 1024], P('blk', 'lev'), may hold values from 0.02 to 0.6
- substeps: int32 [4096], P('blk'), may hold values from 1 to 4
- nest_weight: float32 [4096, 128], P('blk'), may hold values from 0.2 to 0.9
- dest_device: int32 [4096, 1], P('blk'), may hold values from 0 to 63; in each aligned block of 64 rows (0 to 63, 64 to 127, ...) at most 2 rows name the same one
- dest_slot: int32 [4096], P('blk'), may hold values from 0 to 63
- emission_profile: float32 [12], P('lev'), may hold values from 0.05 to 1
- tile_owner: int32 [4096], P('blk'), may hold values from 0 to 1023, as said below
Outputs:
- adjoint_out: float32 [4096, 12, 1024], P('blk', 'lev')
- tile_grad: float32 [1024, 1024], P(('blk', 'lev'))
Inputs may be any that keep to these rules, and one draw needn't show every extreme that they name: Of the 64 blocks of one index of blk, at most 2 have the same dest_device. Tiles form 64 groups of 16 consecutive tiles. Of the 64 blocks of one index of blk, at most 2 have tile_owner in the same group, and some group holds exactly 2 of them.
All inputs are finite; a program needn't handle non-finite values.
Results may differ from a plain program's by a relative error of at most 0.0003.
Values sent between devices are 32-bit elements; how exact they have to be, the bound alone decides.
No kernel may reach another device: no remote copies, remote signals or barrier semaphores. Data moves between devices by JAX's collectives and lax.ppermute only.
A program may use at most 128 MiB of HBM per device.

v0:
```python
import jax
import jax.numpy as jnp
from jax import lax
from jax.sharding import PartitionSpec as P

RMAX = 4
STEPS = 2


def solve_columns(right_side, coupling):
    level_count = right_side.shape[1]
    ratios = []
    scaled = []
    for level in range(level_count):
        lower_k = coupling[:, level - 1] if level > 0 else 0.0
        upper_k = coupling[:, level] if level < level_count - 1 else 0.0
        diag_term = 1.0 + lower_k + upper_k
        if level == 0:
            pivot_val = diag_term
            scaled.append(right_side[:, 0] / pivot_val)
        else:
            pivot_val = diag_term + lower_k * ratios[level - 1]
            scaled.append((right_side[:, level] + lower_k * scaled[level - 1]) / pivot_val)
        ratios.append(-upper_k / pivot_val)
    solved = [None] * level_count
    solved[level_count - 1] = scaled[level_count - 1]
    for level in range(level_count - 2, -1, -1):
        solved[level] = scaled[level] - ratios[level] * solved[level + 1]
    return jnp.stack(solved, axis=1)


def stencil(adjoint, east_u, north_u, side_len):
    shape_grid = adjoint.shape[:-1] + (side_len, side_len)
    grid_view = adjoint.reshape(shape_grid)
    east_c = east_u.reshape(shape_grid)
    north_c = north_u.reshape(shape_grid)
    zero_col = jnp.zeros(shape_grid[:-1] + (1,), jnp.float32)
    east_adj = jnp.concatenate([grid_view[..., 1:], zero_col], axis=-1)
    zero_row = jnp.zeros(shape_grid[:-2] + (1, side_len), jnp.float32)
    north_adj = jnp.concatenate([grid_view[..., 1:, :], zero_row], axis=-2)
    result = (1.0 - east_c - north_c) * grid_view + east_c * east_adj + north_c * north_adj
    return result.reshape(adjoint.shape)


def faces(adjoint, side_len):
    grid_view = adjoint.reshape(adjoint.shape[:-1] + (side_len, side_len))
    return jnp.concatenate(
        [
            grid_view[..., 0, :],
            grid_view[..., side_len - 1, :],
            grid_view[..., :, 0],
            grid_view[..., :, side_len - 1],
        ],
        axis=-1,
    )


def add_faces(adjoint, arrivals, side_len):
    grid_view = adjoint.reshape(adjoint.shape[:-1] + (side_len, side_len))
    grid_view = grid_view.at[..., 0, :].add(arrivals[..., 0:side_len])
    grid_view = grid_view.at[..., side_len - 1, :].add(arrivals[..., side_len : 2 * side_len])
    grid_view = grid_view.at[..., :, 0].add(arrivals[..., 2 * side_len : 3 * side_len])
    grid_view = grid_view.at[..., :, side_len - 1].add(arrivals[..., 3 * side_len :])
    return grid_view.reshape(adjoint.shape)


def route_cycles(cycle_flat, key_float, own_keys):
    all_cycles, all_keys = (
        lax.all_gather(cycle_flat, "blk", axis=0, tiled=True),
        lax.all_gather(key_float[:, None], "blk", axis=0, tiled=True),
    )
    picking = (all_keys[:, 0][None, :] == own_keys[:, None]).astype(jnp.float32)
    return jnp.dot(picking, all_cycles, precision=lax.Precision.HIGHEST)


def local(
    adjoint_in,
    courant,
    mixing,
    oh_rate,
    substeps,
    nest_weight,
    dest_device,
    dest_slot,
    emission_profile,
    tile_owner,
):
    blocks, lev_dev, cell_count = adjoint_in.shape
    cycle_len = nest_weight.shape[1]
    side_len = cycle_len // 4
    peer_count = lax.axis_size("blk")
    lev_groups = lax.axis_size("lev")
    my_block = lax.axis_index("blk")
    survive = jnp.exp(-oh_rate)
    dest_index = dest_device[:, 0]
    key_float = (dest_index * blocks + dest_slot + 1).astype(jnp.float32)
    own_keys = (my_block * blocks + jnp.arange(blocks, dtype=jnp.int32) + 1).astype(jnp.float32)
    column_mixing = lax.all_to_all(mixing, "lev", split_axis=2, concat_axis=1, tiled=True)
    adjoint = adjoint_in
    grad_sum = jnp.zeros((blocks, cell_count), jnp.float32)
    for step_index in range(STEPS):
        grad_sum = grad_sum + jnp.sum(adjoint * emission_profile[None, :, None], axis=1)
        columns = lax.all_to_all(adjoint * survive, "lev", split_axis=2, concat_axis=1, tiled=True)
        solved = solve_columns(columns, column_mixing)
        adjoint = lax.all_to_all(solved, "lev", split_axis=1, concat_axis=2, tiled=True)
        cycle_out = faces(adjoint, side_len) * nest_weight[:, None, :]
        arrivals = route_cycles(cycle_out.reshape(blocks, -1), key_float, own_keys)
        arrivals = arrivals.reshape(cycle_out.shape)
        advected = adjoint
        for substep in range(RMAX):
            active = (substep < substeps)[:, None, None]
            advected = jnp.where(
                active, stencil(advected, courant[0], courant[1], side_len), advected
            )
        adjoint = add_faces(advected, arrivals, side_len)
    tiles_total = blocks * peer_count // 4
    tile_rows = jnp.arange(
        lax.axis_size(("blk", "lev")) * (tiles_total // (peer_count * lev_groups)), dtype=jnp.int32
    )
    tile_hot = (tile_owner[None, :] == tile_rows[:, None]).astype(jnp.float32)
    tile_grad = lax.psum_scatter(
        jnp.dot(tile_hot, grad_sum, precision=lax.Precision.HIGHEST),
        ("blk", "lev"),
        scatter_dimension=0,
        tiled=True,
    )
    return (adjoint, tile_grad)


def solution(mesh):
    placed = (
        P("blk", "lev", None),
        P(None, "blk", "lev", None),
        P("blk", "lev", None),
        P("blk", "lev", None),
        P("blk"),
        P("blk", None),
        P("blk", None),
        P("blk"),
        P("lev"),
        P("blk"),
    )
    return jax.shard_map(
        local,
        mesh=mesh,
        in_specs=placed,
        out_specs=(P("blk", "lev", None), P(("blk", "lev"), None)),
        check_vma=False,
    )
```

profile of v0, /device:TPU:1, one launch (start us, length us, event | category | flops | bytes accessed | tf_op | source)
XLA Modules:
  0.0 777.3 jit_solution(1277644381630115909)
XLA Ops:
  11.6 5.0 all-to-all-start.1
  22.7 4.0 all-to-all-done.1
  26.8 4.2 all-to-all-start
  31.5 2.9 reduce.17
  36.3 3.8 all-to-all-done
  40.2 4.7 reduce.18
  61.2 3.5 all-to-all-start.2
  64.9 8.1 %all-to-all-done.2 = f32[64,12,256]{2,0,1:T(8,128)S(1)} async-done(((f32[64,12,256]{2,0,1:T(8,128)}), f32[64,12,256]{2,0,1:T(8,128)S(1)}, u32[]{:S(2)}, u32[]{:S(2)}) %all-to-all-start.2) | async-done | bytes 786464 | tf_op jit(solution)/shard_map/all_to_all | solution.py:105
  80.6 264.6 %all-reduce.16 = f32[4096]{0:T(1024)S(1)} all-reduce(f32[4096]{0:T(1024)S(1)} %fusion.43), channel_id=2, replica_groups=mesh['blk'=64,'lev'=4] {'blk'}, use_global_device_ids=true, to_apply=%add.16 | all-reduce | flops 4096 | bytes 32768
  353.7 5.8 fusion.2
  370.6 2.7 scatter-add.30
  374.4 2.8 scatter-add.31
  377.1 2.7 copy.173
  382.3 2.7 copy.174
  384.9 4.3 reshape.377
  389.2 4.2 all-to-all-start.3
  398.0 4.9 fusion.10
  403.0 4.7 reduce.19
  407.7 3.7 reshape.378
  418.7 13.0 %all_to_all.84 = f32[64,12,256]{2,0,1:T(8,128)} all-to-all(f32[64,12,256]{2,0,1:T(8,128)S(1)} %constant_dynamic-update-slice_fusion.11), channel_id=1, replica_groups=mesh['blk'=64,'lev'=4] {'lev'}, dimensions={1} | all-to-all | bytes 1572864 | tf_op jit(solution)/shard_map/all_to_all | solution.py:105
  431.8 2.8 copy.177
  447.7 223.3 %all-reduce.20.cloned.1.call-done = f32[1024,1024]{1,0:T(8,128)} async-done(((f32[1024,1024]{1,0:T(8,128)}), f32[1024,1024]{1,0:T(8,128)}) %all-reduce.20.cloned.1.call-update) | async-done | bytes 4194320
  672.4 83.4 %all-gather.6.cloned.1.call-done = f32[4096,384]{1,0:T(8,128)} async-done(((f32[64,384]{1,0:T(8,128)}), f32[4096,384]{1,0:T(8,128)}) %all-gather.6.cloned.1.call-update) | async-done | bytes 6291472 | tf_op jit(solution)/shard_map/all_gather | solution.py:69
  755.8 7.8 %fusion = f32[64,384]{0,1:T(8,128)S(1)} fusion(f32[4096,384]{1,0:T(8,128)} %all-gather.6.cloned.1.call-done, f32[4096]{0:T(1024)S(1)} %all-reduce.16, f32[64]{0:T(128)S(1)} %copy-done.33), kind=kOutput, calls=%fused_computation.10 | convolution fusion | flops 1208221696 | bytes 6406400 | tf_op jit(solution)/shard_map/reshape | solution.py:108
  (191 shorter events, 92.0 us)
Async XLA Ops:
  9.0 7.5 copy-start.34
  11.6 5.0 copy-start.6
  11.6 5.0 copy-start.19
  11.6 15.2 %all-to-all-start.1 = ((f32[4,1,49152]{2,1,0:T(1,128)}), f32[4,1,49152]{2,1,0:T(1,128)S(1)}, u32[]{:S(2)}, u32[]{:S(2)}) async-start(f32[4,1,49152]{2,1,0:T(1,128)} %reshape.373), calls=%async_computation.1 | async-start | bytes 1572864 | tf_op jit(solution)/shard_map/all_to_all | solution.py:98
  26.8 13.4 %all-to-all-start = ((f32[4,1,49152]{2,1,0:T(1,128)}), f32[4,1,49152]{2,1,0:T(1,128)}, u32[]{:S(2)}, u32[]{:S(2)}) async-start(f32[4,1,49152]{2,1,0:T(1,128)} %reshape.375), calls=%async_computation | async-start | bytes 1572864 | tf_op jit(solution)/shard_map/all_to_all | solution.py:103
  36.3 23.4 %copy-start.3 = (f32[64,4,3,256]{3,0,2,1:T(8,128)}, f32[64,4,3,256]{3,0,2,1:T(8,128)S(1)}, u32[]{:S(2)}) copy-start(f32[64,4,3,256]{3,0,2,1:T(8,128)S(1)} %copy.164) | copy-start | bytes 2359300
  50.6 4.4 copy-start.7
  50.6 4.4 copy-start.9
  55.0 9.7 %copy-start.23 = (f32[64,128]{1,0:T(8,128)S(1)}, f32[64,128]{1,0:T(8,128)}, u32[]{:S(2)}) copy-start(f32[64,128]{1,0:T(8,128)} %param.31) | copy-start | bytes 98308
  61.2 11.8 %all-to-all-start.2 = ((f32[64,12,256]{2,0,1:T(8,128)}), f32[64,12,256]{2,0,1:T(8,128)S(1)}, u32[]{:S(2)}, u32[]{:S(2)}) async-start(f32[64,12,256]{2,0,1:T(8,128)} %constant_dynamic-update-slice_fusion), calls=%async_computation.2 | async-start | bytes 1572864 | tf_op jit(solution)/shard_map/all_to_all | solution.py:105
  64.7 288.9 %all-gather.4.cloned.1.call-start = ((), (), s32[]{:S(2)}) async-start(), calls=%async_computation.5 | async-start | bytes 6389760 | tf_op jit(solution)/shard_map/all_gather | solution.py:69
  64.9 8.8 %copy-start.20 = (f32[64,128]{0,1:T(8,128)}, f32[64,128]{0,1:T(8,128)S(1)}, u32[]{:S(2)}) copy-start(f32[64,128]{0,1:T(8,128)S(1)} %copy.167) | copy-start | bytes 98308
  77.7 267.5 %copy-start.37 = (s32[64]{0:T(128)S(1)}, s32[64]{0:T(128)}, u32[]{:S(2)}) copy-start(s32[64]{0:T(128)} %param.30) | copy-start | bytes 772
  345.2 8.5 %copy-start.32 = (f32[64]{0:T(128)}, f32[64]{0:T(128)S(1)}, u32[]{:S(2)}) copy-start(f32[64]{0:T(128)S(1)} %add_convert_fusion) | copy-start | bytes 772
  345.2 4.9 copy-start.26
  345.2 6.3 copy-start.24
  384.9 8.6 %copy-start.35 = (f32[3]{0:T(128)S(1)}, f32[3]{0:T(128)}, u32[]{:S(2)}) copy-start(f32[3]{0:T(128)} %param.34) | copy-start | bytes 40
  389.2 13.7 %all-to-all-start.3 = ((f32[4,1,49152]{2,1,0:T(1,128)}), f32[4,1,49152]{2,1,0:T(1,128)}, u32[]{:S(2)}, u32[]{:S(2)}) async-start(f32[4,1,49152]{2,1,0:T(1,128)} %reshape.377), calls=%async_computation.3 | async-start | bytes 1572864 | tf_op jit(solution)/shard_map/all_to_all | solution.py:103
  393.5 4.5 copy-start.36
  393.5 277.5 %all-reduce.20.cloned.1.call-start = ((), (), s32[]{:S(2)}) async-start(), calls=%async_computation.7 | async-start | bytes 8388608
  402.9 352.8 %all-gather.6.cloned.1.call-start = ((), (), s32[]{:S(2)}) async-start(), calls=%async_computation.6 | async-start | bytes 6389760 | tf_op jit(solution)/shard_map/all_gather | solution.py:69
  431.8 4.8 copy-start.21
  445.5 310.2 %copy-start.33 = (f32[64]{0:T(128)S(1)}, f32[64]{0:T(128)}, u32[]{:S(2)}) copy-start(f32[64]{0:T(128)} %copy-done.32) | copy-start | bytes 772
  672.3 91.3 %copy-start.5 = (f32[64,3,32,32]{0,3,2,1:T(8,128)S(1)}, f32[64,3,32,32]{0,3,2,1:T(8,128)}, u32[]{:S(2)}) copy-start(f32[64,3,32,32]{0,3,2,1:T(8,128)} %add_select_fusion) | copy-start | bytes 2359300
  (24 other events, 55.2 us)
Sparse Core Ops, SparseCore 0:
  74.8 88.7 all-gather.3
  403.1 267.8 all-reduce.19
  674.3 81.4 all-gather.5
where the time goes:
time: 788 us; the launch traced here: 777 us
  waiting for transfers between devices  323 us (41%)
  blocking collectives  278 us (35%)
  local copies, waits for them, and re-layouts  77.4 us (10%)
  other arithmetic  48.5 us (6%)
  matrix products  18.5 us (2%)
  starting transfers between devices  17 us (2%)
  between operations  15.5 us (2%)
    unnamed x1, blocking collectives  265 us
    unnamed x4, waiting for transfers between devices  223 us
    all_gather x2, waiting for transfers between devices, route_cycles(): lax.all_gather(cycle_flat, 'blk', axis=0, tiled=True)  83.4 us
    unnamed x108, local copies, waits for them, and re-layouts  31.9 us
  transfers between devices with their start and end apart: 7, of which 5 were waited for; matrix products, arithmetic and copies ran while one was open for 8% of the time, Pallas kernels for 0%

commit v1 on v0

--- a/solution.py
+++ b/solution.py
@@ -66,7 +66,9 @@
 
 def route_cycles(cycle_flat, key_float, own_keys):
     all_cycles, all_keys = (
-        lax.all_gather(cycle_flat, "blk", axis=0, tiled=True),
+        jnp.concatenate(
+            lax.all_to_all(jnp.stack([cycle_flat] * lax.axis_size("blk")), "blk", 0, 0), axis=0
+        ),
         lax.all_gather(key_float[:, None], "blk", axis=0, tiled=True),
     )
     picking = (all_keys[:, 0][None, :] == own_keys[:, None]).astype(jnp.float32)

time: 788 us -> 1040 us (1.32)
  local copies, waits for them, and re-layouts: 77.4 us -> 184 us
  blocking collectives: 278 us -> 383 us
  other arithmetic: 48.5 us -> 79.6 us
  starting transfers between devices: 17 us -> 46.8 us
  waiting for transfers between devices: 323 us -> 300 us
    unnamed x1, blocking collectives: 265 us -> 358 us
    all_gather x2 -> x0, waiting for transfers between devices: 83.4 us -> none  [route_cycles(): lax.all_gather(cycle_flat, 'blk', axis=0, tiled=True)]
    unnamed x4 -> x2, waiting for transfers between devices: 223 us -> 285 us
    scatter-add x2 -> x4, local copies, waits for them, and re-layouts: 5.34 us -> 58.1 us  [the longest x2 34.9 us: add_faces(): grid_view.at[..., side_len - 1, :].add(arrivals[..., side_len:2 * side_len])]
    all_to_all x0 -> x2, starting transfers between devices: none -> 34.3 us  [route_cycles(): lax.all_to_all(jnp.stack([cycle_flat] * lax.axis_size('blk')), 'blk', 0, 0)]
    another operation x0 -> x10, local copies, waits for them, and re-layouts: none -> 29.2 us
    add x4, other arithmetic: 2.27 us -> 19.8 us  [the longest x2 9.93 us: add_faces(): grid_view = grid_view.at[..., 0, :].add(arrivals[..., 0:side_len])]
    dot_general x0 -> x2, local copies, waits for them, and re-layouts: none -> 13.2 us  [route_cycles(): return jnp.dot(picking, all_cycles, precision=lax.Precision.HIGHEST)]
  transfers between devices with their start and end apart: 7 -> 6, of which waited for: 5 -> 4; matrix products, arithmetic and copies ran while one was open for 8% -> 8% of each run, Pallas kernels for 0% -> 0%
where the time goes in v1:
time: 1040 us; the launch traced here: 1030 us
  blocking collectives  383 us (37%)
  waiting for transfers between devices  300 us (29%)
  local copies, waits for them, and re-layouts  184 us (18%)
  other arithmetic  79.6 us (8%)
  starting transfers between devices  46.8 us (4%)
  matrix products  17.1 us (2%)
  between operations  15.6 us (2%)
    unnamed x1, blocking collectives  358 us
    unnamed x2, waiting for transfers between devices  285 us
    scatter-add x2, local copies, waits for them, and re-layouts, add_faces(): grid_view.at[..., side_len - 1, :].add(arrivals[..., side_len:2 * side_len])  34.9 us
    all_to_all x2, starting transfers between devices, route_cycles(): lax.all_to_all(jnp.stack([cycle_flat] * lax.axis_size('blk')), 'blk', 0, 0)  34.3 us
    unnamed x70, local copies, waits for them, and re-layouts  33.4 us
    scatter-add x2, local copies, waits for them, and re-layouts, add_faces(): grid_view = grid_view.at[..., 0, :].add(arrivals[..., 0:side_len])  23.3 us
  transfers between devices with their start and end apart: 6, of which 4 were waited for; matrix products, arithmetic and copies ran while one was open for 8% of the time, Pallas kernels for 0%

profile of v1, /device:TPU:1, one launch (start us, length us, event | category | flops | bytes accessed | tf_op | source)
XLA Modules:
  0.0 1026.0 jit_solution(12724613031366319189)
XLA Ops:
  11.6 4.8 all-to-all-start.1
  40.0 4.8 reduce.18
  64.7 8.2 all-to-all-done.2
  77.0 21.2 %all-to-all-start.3 = ((f32[64,64,384]{2,1,0:T(8,128)}), f32[64,64,384]{2,1,0:T(8,128)}, u32[]{:S(2)}, u32[]{:S(2)}) async-start(f32[64,64,384]{2,1,0:T(8,128)} %stack.9), calls=%async_computation.3 | async-start | bytes 12582912 | tf_op jit(solution)/shard_map/all_to_all | solution.py:70
  110.7 358.2 %all-reduce.16 = f32[4096]{0:T(1024)S(1)} all-reduce(f32[4096]{0:T(1024)S(1)} %fusion.47), channel_id=2, replica_groups=mesh['blk'=64,'lev'=4] {'blk'}, use_global_device_ids=true, to_apply=%add.16 | all-reduce | flops 4096 | bytes 32768
  491.0 6.6 copy.283
  497.6 6.2 fusion.2
  508.9 4.4 copy.287
  513.3 5.4 slice_add_fusion.3
  518.8 8.3 scatter-add.26
  527.1 5.4 slice_add_fusion.2
  532.5 12.5 %scatter-add.29 = f32[64,3,32,32]{2,0,1,3:T(8,128)} dynamic-update-slice(f32[64,3,32,32]{2,0,1,3:T(8,128)} %scatter-add.26, f32[64,3,1,32]{2,0,1,3:T(8,128)} %slice_add_fusion.2, s32[]{:T(128)} %constant.203.clone.1, s32[]{:T(128)} %constant.203.clone.1, s32[]{:T(128)} %constant.208.clone.1, s32[]{:T(128)} %constant.203.clone.1) | dynamic-update-slice | bytes 49156 | tf_op jit(solution)/shard_map/scatter-add | solution.py:61
  563.7 13.0 %all_to_all.94 = f32[4,1,49152]{2,1,0:T(1,128)} all-to-all(f32[4,1,49152]{2,1,0:T(1,128)} %reshape.386), channel_id=1, replica_groups=mesh['blk'=64,'lev'=4] {'lev'}, dimensions={0} | all-to-all | bytes 1572864 | tf_op jit(solution)/shard_map/all_to_all | solution.py:105
  576.7 4.7 reduce.19
  592.7 11.5 %all_to_all.95 = f32[64,12,256]{2,0,1:T(8,128)} all-to-all(f32[64,12,256]{2,0,1:T(8,128)S(1)} %constant_dynamic-update-slice_fusion.11), channel_id=1, replica_groups=mesh['blk'=64,'lev'=4] {'lev'}, dimensions={1} | all-to-all | bytes 1572864 | tf_op jit(solution)/shard_map/all_to_all | solution.py:107
  613.3 13.0 %all-to-all-start.6 = ((f32[64,64,384]{2,1,0:T(8,128)}), f32[64,64,384]{2,1,0:T(8,128)}, u32[]{:S(2)}, u32[]{:S(2)}) async-start(f32[64,64,384]{2,1,0:T(8,128)} %stack.11), calls=%async_computation.6 | async-start | bytes 12582912 | tf_op jit(solution)/shard_map/all_to_all | solution.py:70
  633.6 4.7 fusion.12
  660.5 285.4 %all-reduce.20.cloned.1.call-done = f32[1024,1024]{1,0:T(8,128)} async-done(((f32[1024,1024]{1,0:T(8,128)}), f32[1024,1024]{1,0:T(8,128)}) %all-reduce.20.cloned.1.call-update) | async-done | bytes 4194320
  947.3 6.6 copy.311
  953.9 6.2 fusion
  963.8 4.5 slice_add_fusion.1
  968.3 14.9 %scatter-add.34 = f32[64,3,32,32]{2,0,1,3:T(8,128)S(1)} dynamic-update-slice(f32[64,3,32,32]{2,0,1,3:T(8,128)S(1)} %copy-done.2, f32[64,3,1,32]{2,0,1,3:T(8,128)} %slice_add_fusion.1, s32[]{:T(128)} %constant.203.clone.1, s32[]{:T(128)} %constant.203.clone.1, s32[]{:T(128)} %constant.203.clone.1, s32[]{:T(128)} %constant.203.clone.1) | dynamic-update-slice | bytes 49156 | tf_op jit(solution)/shard_map/scatter-add | solution.py:60
  986.9 4.4 slice_add_fusion
  991.3 22.4 %scatter-add.35 = f32[64,3,32,32]{2,0,1,3:T(8,128)S(1)} dynamic-update-slice(f32[64,3,32,32]{2,0,1,3:T(8,128)S(1)} %scatter-add.34, f32[64,3,1,32]{2,0,1,3:T(8,128)} %slice_add_fusion, s32[]{:T(128)} %constant.203.clone.1, s32[]{:T(128)} %constant.203.clone.1, s32[]{:T(128)} %constant.208.clone.1, s32[]{:T(128)} %constant.203.clone.1) | dynamic-update-slice | bytes 49156 | tf_op jit(solution)/shard_map/scatter-add | solution.py:61
  (164 shorter events, 172.8 us)
Async XLA Ops:
  7.2 9.2 copy-start.17
  11.6 15.1 %all-to-all-start.1 = ((f32[4,1,49152]{2,1,0:T(1,128)}), f32[4,1,49152]{2,1,0:T(1,128)S(1)}, u32[]{:S(2)}, u32[]{:S(2)}) async-start(f32[4,1,49152]{2,1,0:T(1,128)} %reshape.382), calls=%async_computation.1 | async-start | bytes 1572864 | tf_op jit(solution)/shard_map/all_to_all | solution.py:100
  26.6 13.4 %all-to-all-start = ((f32[4,1,49152]{2,1,0:T(1,128)}), f32[4,1,49152]{2,1,0:T(1,128)}, u32[]{:S(2)}, u32[]{:S(2)}) async-start(f32[4,1,49152]{2,1,0:T(1,128)} %reshape.384), calls=%async_computation | async-start | bytes 1572864 | tf_op jit(solution)/shard_map/all_to_all | solution.py:105
  36.2 23.4 %copy-start.5 = (f32[64,4,3,256]{3,0,2,1:T(8,128)}, f32[64,4,3,256]{3,0,2,1:T(8,128)S(1)}, u32[]{:S(2)}) copy-start(f32[64,4,3,256]{3,0,2,1:T(8,128)S(1)} %copy.266) | copy-start | bytes 2359300
  50.5 10.5 %copy-start.7 = (f32[64,1,256]{2,0,1:T(8,128)}, f32[64,1,256]{2,0,1:T(8,128)S(1)}, u32[]{:S(2)}) copy-start(f32[64,1,256]{2,0,1:T(8,128)S(1)} %get-tuple-element.150) | copy-start | bytes 196612
  50.5 10.5 %copy-start.10 = (f32[64,1,256]{2,0,1:T(8,128)}, f32[64,1,256]{2,0,1:T(8,128)S(1)}, u32[]{:S(2)}) copy-start(f32[64,1,256]{2,0,1:T(8,128)S(1)} %get-tuple-element.134) | copy-start | bytes 196612
  50.5 10.5 %copy-start.11 = (f32[64,1,256]{2,0,1:T(8,128)}, f32[64,1,256]{2,0,1:T(8,128)S(1)}, u32[]{:S(2)}) copy-start(f32[64,1,256]{2,0,1:T(8,128)S(1)} %get-tuple-element.139) | copy-start | bytes 196612
  50.5 10.5 %copy-start.12 = (f32[64,1,256]{2,0,1:T(8,128)}, f32[64,1,256]{2,0,1:T(8,128)S(1)}, u32[]{:S(2)}) copy-start(f32[64,1,256]{2,0,1:T(8,128)S(1)} %get-tuple-element.144) | copy-start | bytes 196612
  50.5 10.5 %copy-start.13 = (f32[64,1,256]{2,0,1:T(8,128)}, f32[64,1,256]{2,0,1:T(8,128)S(1)}, u32[]{:S(2)}) copy-start(f32[64,1,256]{2,0,1:T(8,128)S(1)} %get-tuple-element.149) | copy-start | bytes 196612
  50.5 10.5 %copy-start.14 = (f32[64,1,256]{2,0,1:T(8,128)}, f32[64,1,256]{2,0,1:T(8,128)S(1)}, u32[]{:S(2)}) copy-start(f32[64,1,256]{2,0,1:T(8,128)S(1)} %get-tuple-element.154) | copy-start | bytes 196612
  50.6 14.0 %copy-start.16 = (f32[64,128]{1,0:T(8,128)S(1)}, f32[64,128]{1,0:T(8,128)}, u32[]{:S(2)}) copy-start(f32[64,128]{1,0:T(8,128)} %param.31) | copy-start | bytes 98308
  61.0 11.8 %all-to-all-start.2 = ((f32[64,12,256]{2,0,1:T(8,128)}), f32[64,12,256]{2,0,1:T(8,128)S(1)}, u32[]{:S(2)}, u32[]{:S(2)}) async-start(f32[64,12,256]{2,0,1:T(8,128)} %constant_dynamic-update-slice_fusion), calls=%async_computation.2 | async-start | bytes 1572864 | tf_op jit(solution)/shard_map/all_to_all | solution.py:107
  64.7 12.3 %copy-start.15 = (f32[64,128]{0,1:T(8,128)}, f32[64,128]{0,1:T(8,128)S(1)}, u32[]{:S(2)}) copy-start(f32[64,128]{0,1:T(8,128)S(1)} %copy.281) | copy-start | bytes 98308
  77.0 21.3 %copy-start.9 = (f32[2,64,3,1024]{3,1,2,0:T(8,128)S(1)}, f32[2,64,3,1024]{3,1,2,0:T(8,128)}, u32[]{:S(2)}) copy-start(f32[2,64,3,1024]{3,1,2,0:T(8,128)} %param.27) | copy-start | bytes 4718596
  77.0 414.0 %all-to-all-start.3 = ((f32[64,64,384]{2,1,0:T(8,128)}), f32[64,64,384]{2,1,0:T(8,128)}, u32[]{:S(2)}, u32[]{:S(2)}) async-start(f32[64,64,384]{2,1,0:T(8,128)} %stack.9), calls=%async_computation.3 | async-start | bytes 12582912 | tf_op jit(solution)/shard_map/all_to_all | solution.py:70
  103.1 6.1 copy-start.22
  103.1 7.4 copy-start.20
  103.2 7.4 copy-start.21
  103.2 365.8 %copy-start.19 = (s32[64]{0:T(128)S(1)}, s32[64]{0:T(128)}, u32[]{:S(2)}) copy-start(s32[64]{0:T(128)} %param.30) | copy-start | bytes 772
  472.3 3.8 slice-start.1
  585.1 4.2 copy-start.8
  613.3 334.0 %all-to-all-start.6 = ((f32[64,64,384]{2,1,0:T(8,128)}), f32[64,64,384]{2,1,0:T(8,128)}, u32[]{:S(2)}, u32[]{:S(2)}) async-start(f32[64,64,384]{2,1,0:T(8,128)} %stack.11), calls=%async_computation.6 | async-start | bytes 12582912 | tf_op jit(solution)/shard_map/all_to_all | solution.py:70
  626.3 319.6 %all-reduce.20.cloned.1.call-start = ((), (), s32[]{:S(2)}) async-start(), calls=%async_computation.7 | async-start | bytes 8388608
  626.4 7.2 copy-start.18
  (7 other events, 21.2 us)
Sparse Core Ops, SparseCore 0:
  638.4 307.4 all-reduce.19
